TPU v7x, 512 devices: a whole 4x8x8 slice. The times are simulated.
512 devices in a mesh: shift: 4 (over x_hi, core), space: 128 (over y, z, x_lo).
Axes of the slice: x: 4 (x_hi: 2, x_lo: 2; x = x_hi * 2 + x_lo), y: 8, z: 8, core: 2. Of those that a mesh axis runs over, the one named last changes fastest.
Arguments:
- labels: int32 [256, 32, 256], P('space'), may hold values from 0 to 7
- conductance: float32 [8], replicated, may hold values from 0.2 to 5
- capacity_table: float32 [8], replicated, may hold values from 0.5 to 2
- shift_values: float32 [8], replicated, may hold values from 0.1 to 4
- prior_basis: float32 [256, 256, 32, 256], P(None, 'space', 'shift'), may hold values from -6 to 6
Outputs:
- new_block: float32 [8, 8, 256, 32, 256], P(None, None, 'space', 'shift')
- coefficients: float32 [64, 256], replicated
- factor: float32 [64, 64], replicated
All inputs are finite; a program needn't handle non-finite values.
Results may differ from a plain program's by a relative error of at most 0.0003.
Values sent between devices are 32-bit elements; how exact they have to be, the bound alone decides.
No kernel may reach another device: no remote copies, remote signals or barrier semaphores. Data moves between devices by JAX's collectives and lax.ppermute only.
A program may use at most 64 MiB of HBM per device.

v0:
```python
import jax
import jax.numpy as jnp
from jax import lax
from jax.sharding import PartitionSpec as P

COLS = 8
SWEEPS = 4
LOWER_BOUND = 0.1
UPPER_BOUND = 2.0


def padded_2(cells, sides, width):
    for axis, dim in sides:
        count = lax.axis_size(axis)
        ends = count - 1
        head = lax.slice_in_dim(cells, 0, width, axis=dim)
        tail = lax.slice_in_dim(cells, cells.shape[dim] - width, cells.shape[dim], axis=dim)
        cells = jnp.concatenate(
            [
                lax.ppermute(tail, axis, [(i, (i + 1) % count) for i in range(ends)]),
                cells,
                lax.ppermute(head, axis, [((i + 1) % count, i) for i in range(ends)]),
            ],
            axis=dim,
        )
    return cells


def lookup(labels, table):
    materials = jnp.arange(table.shape[0], dtype=jnp.int32)
    onehot = (labels[None] == materials[:, None, None, None]).astype(jnp.float32)
    return jnp.sum(onehot * table[:, None, None, None], axis=0)


def conductances(conduct, padded):
    west_face = 0.5 * (conduct + padded[:-2, 1:-1, 1:-1])
    east_face = 0.5 * (conduct + padded[2:, 1:-1, 1:-1])
    south_face = 0.5 * (conduct + padded[1:-1, :-2, 1:-1])
    north_face = 0.5 * (conduct + padded[1:-1, 2:, 1:-1])
    below_face = 0.5 * (conduct + padded[1:-1, 1:-1, :-2])
    above_face = 0.5 * (conduct + padded[1:-1, 1:-1, 2:])
    return (west_face, east_face, south_face, north_face, below_face, above_face)


def neighbours(padded, face_list):
    west_face, east_face, south_face, north_face, below_face, above_face = face_list
    summed = west_face * padded[..., :-2, 1:-1, 1:-1] + east_face * padded[..., 2:, 1:-1, 1:-1]
    summed = (
        summed
        + south_face * padded[..., 1:-1, :-2, 1:-1]
        + north_face * padded[..., 1:-1, 2:, 1:-1]
    )
    summed = (
        summed
        + below_face * padded[..., 1:-1, 1:-1, :-2]
        + above_face * padded[..., 1:-1, 1:-1, 2:]
    )
    return summed


def diagonal_of(face_list, shift_list, capacity):
    west_face, east_face, south_face, north_face, below_face, above_face = face_list
    summed = west_face + east_face + (south_face + north_face) + (below_face + above_face)
    return summed[None, None] + shift_list[:, None, None, None, None] * capacity[None, None]


def chebyshev(source, face_list, diagonal, padder):
    center = 0.5 * (UPPER_BOUND + LOWER_BOUND)
    spread = 0.5 * (UPPER_BOUND - LOWER_BOUND)
    ratio_value = center / spread
    reciprocal = 1.0 / diagonal
    solution = jnp.zeros_like(source)
    remainder = source
    weight_old = 1.0 / ratio_value
    direction = reciprocal * remainder / center
    for sweep_index in range(SWEEPS):
        solution = solution + direction
        if sweep_index + 1 < SWEEPS:
            applied = diagonal * direction - neighbours(padder(direction), face_list)
            remainder = remainder - applied
            weight_new = 1.0 / (2.0 * ratio_value - weight_old)
            direction = weight_new * weight_old * direction + 2.0 * weight_new / spread * (
                reciprocal * remainder
            )
            weight_old = weight_new
    return solution


def products(left_side, right_side):
    return lax.dot_general(
        left_side, right_side, (((1,), (1,)), ((), ())), precision=lax.Precision.HIGHEST
    )


def matmul(left_side, right_side):
    return jnp.dot(left_side, right_side, precision=lax.Precision.HIGHEST)


def local(labels, conductance, capacity_table, shift_values, prior_basis):
    groups = lax.axis_size("shift")
    shifts_all = shift_values.shape[0]
    per_device = shifts_all // groups
    new_count = shifts_all * COLS
    basis_count = prior_basis.shape[0]
    slab_x = prior_basis.shape[1]
    quarter = prior_basis.shape[2]
    depth = prior_basis.shape[3]
    flat_basis = prior_basis.reshape(basis_count, slab_x * quarter * depth)
    cell_weight = 1.0 / (slab_x * quarter * depth * groups * lax.axis_size("space"))
    tail_columns = prior_basis[basis_count - new_count :]
    conduct = lookup(labels, conductance)
    capacity = lookup(labels, capacity_table)
    rimmed = padded_2(conduct, (("space", 0),), 1)
    face_list = conductances(conduct, jnp.pad(rimmed, ((0, 0), (1, 1), (1, 1))))
    shift_list = lax.dynamic_slice_in_dim(
        shift_values, lax.axis_index("shift") * per_device, per_device, 0
    )
    diagonal = diagonal_of(face_list, shift_list, capacity)
    starting = lax.all_to_all(tail_columns, "shift", split_axis=0, concat_axis=2, tiled=True)
    full_y = starting.shape[2]
    source = starting.reshape(per_device, COLS, slab_x, full_y, depth) * capacity[None, None]

    def padder(field):
        widened = padded_2(field, (("space", 2),), 1)
        return jnp.pad(widened, ((0, 0), (0, 0), (0, 0), (1, 1), (1, 1)))

    fields = chebyshev(source, face_list, diagonal, padder)
    merged = fields.reshape(per_device * COLS, slab_x, full_y, depth)
    regrouped = lax.all_to_all(merged, "shift", split_axis=2, concat_axis=0, tiled=True)
    columns = regrouped.reshape(new_count, slab_x * quarter * depth)
    first_proj = lax.psum(products(columns, flat_basis), ("shift", "space")) * cell_weight
    columns = columns - matmul(first_proj, flat_basis)
    second_proj = lax.psum(products(columns, flat_basis), ("shift", "space")) * cell_weight
    columns = columns - matmul(second_proj, flat_basis)
    gram_matrix = lax.psum(products(columns, columns), ("shift", "space")) * cell_weight
    factor = jnp.linalg.cholesky(gram_matrix)
    orthonormal = lax.linalg.triangular_solve(factor, columns, left_side=True, lower=True)
    new_block = orthonormal.reshape(shifts_all, COLS, slab_x, quarter, depth)
    return (new_block, first_proj + second_proj, factor)


def solution(mesh):
    in_specs = (P("space", None, None), P(), P(), P(), P(None, "space", "shift", None))
    out_specs = (P(None, None, "space", "shift", None), P(), P())
    return jax.shard_map(local, mesh=mesh, in_specs=in_specs, out_specs=out_specs, check_vma=False)
```

profile of v0, /device:TPU:1, one launch (start us, length us, event | category | flops | bytes accessed | tf_op | source)
XLA Modules:
  0.0 803.1 jit_solution(15233755541338323633)
XLA Ops:
  7.2 2.3 slice.133
  9.5 10.4 %all-to-all-start = ((f32[64,2,8,256]{3,2,1,0:T(8,128)}), f32[64,2,8,256]{3,2,1,0:T(8,128)S(1)}, u32[]{:S(2)}, u32[]{:S(2)}) async-start(f32[64,2,8,256]{3,2,1,0:T(8,128)} %slice.133), calls=%async_computation | async-start | bytes 2097152 | tf_op jit(solution)/shard_map/all_to_all | solution.py:119
  19.9 0.2 select_reduce_fusion.1
  20.1 1.3 collective-permute-start
  21.4 1.3 collective-permute-start.1
  22.7 0.1 dynamic_slice.3
  22.8 10.3 %collective-permute-done = f32[1,32,256]{2,1,0:T(8,128)S(1)} collective-permute-done((f32[1,32,256]{2,1,0:T(8,128)S(1)}, f32[1,32,256]{2,1,0:T(8,128)S(1)}, u32[]{:S(2)}, u32[]{:S(2)}) %collective-permute-start) | collective-permute-done | bytes 32800 | tf_op jit(solution)/shard_map/ppermute | solution.py:20
  33.0 0.0 collective-permute-done.1
  33.0 0.1 select_maximum_fusion.6
  33.2 0.1 add_add_fusion
  33.3 0.1 multiply_add_fusion.2
  33.4 2.3 all-to-all-done
  35.7 0.1 copy.35
  35.8 0.2 fusion.37
  36.0 0.1 fusion.69
  36.1 1.9 collective-permute-start.2
  37.9 1.3 collective-permute-start.3
  39.2 20.6 %collective-permute-done.2 = f32[2,8,1,32,256]{4,3,2,1,0:T(8,128)S(1)} collective-permute-done((f32[2,8,1,32,256]{4,3,2,1,0:T(8,128)S(1)}, f32[2,8,1,32,256]{4,3,2,1,0:T(8,128)S(1)}, u32[]{:S(2)}, u32[]{:S(2)}) %collective-permute-start.2) | collective-permute-done | bytes 524320 | tf_op jit(solution)/shard_map/ppermute | solution.py:20
  59.8 0.0 collective-permute-done.3
  59.8 1.8 select_maximum_fusion.4
  61.6 1.2 multiply_add_fusion.1
  62.8 0.1 fusion.68
  62.9 4.1 collective-permute-start.4
  67.1 1.3 collective-permute-start.5
  68.4 19.6 %collective-permute-done.4 = f32[2,8,1,32,256]{4,3,2,1,0:T(8,128)S(1)} collective-permute-done((f32[2,8,1,32,256]{4,3,2,1,0:T(8,128)S(1)}, f32[2,8,1,32,256]{4,3,2,1,0:T(8,128)S(1)}, u32[]{:S(2)}, u32[]{:S(2)}) %collective-permute-start.4) | collective-permute-done | bytes 524320 | tf_op jit(solution)/shard_map/ppermute | solution.py:20
  88.0 0.0 collective-permute-done.5
  88.0 1.8 select_maximum_fusion.2
  89.8 1.2 multiply_add_fusion
  91.0 0.1 fusion.67
  91.1 4.1 collective-permute-start.6
  95.3 1.3 collective-permute-start.7
  96.6 18.6 %collective-permute-done.6 = f32[2,8,1,32,256]{4,3,2,1,0:T(8,128)S(1)} collective-permute-done((f32[2,8,1,32,256]{4,3,2,1,0:T(8,128)S(1)}, f32[2,8,1,32,256]{4,3,2,1,0:T(8,128)S(1)}, u32[]{:S(2)}, u32[]{:S(2)}) %collective-permute-start.6) | collective-permute-done | bytes 524320 | tf_op jit(solution)/shard_map/ppermute | solution.py:20
  115.1 0.0 collective-permute-done.7
  115.1 1.8 select_maximum_fusion
  117.0 1.4 fusion.9
  118.3 1.8 copy.36
  120.1 6.9 all-to-all-start.1
  127.0 0.0 all-reduce.7.cloned.1.call-start
  127.0 7.9 copy.46
  135.0 7.2 all-to-all-done.1
  142.1 0.6 copy.53
  142.8 0.1 copy.38
  142.9 0.2 reshape.60
  143.1 6.8 fusion.71
  149.9 0.0 all-reduce.7.cloned.1.call-update
  149.9 0.3 all-reduce.9.cloned.1.call-start
  150.2 267.6 %all-reduce.7.cloned.1.call-done = f32[64,256]{1,0:T(8,128)} async-done(((f32[64,256]{1,0:T(8,128)}), f32[64,256]{1,0:T(8,128)}) %all-reduce.7.cloned.1.call-update) | async-done | bytes 65552 | tf_op jit(solution)/shard_map/psum | solution.py:131
  417.8 5.0 convolution_subtract_fusion.1
  422.7 4.6 fusion.72
  427.3 0.0 all-reduce.9.cloned.1.call-update
  427.4 251.4 %all-reduce.9.cloned.1.call-done = f32[64,256]{1,0:T(8,128)} async-done(((f32[64,256]{1,0:T(8,128)}), f32[64,256]{1,0:T(8,128)}) %all-reduce.9.cloned.1.call-update) | async-done | bytes 65552 | tf_op jit(solution)/shard_map/psum | solution.py:133
  678.8 4.8 convolution_subtract_fusion
  683.6 1.0 fusion.73
  684.6 94.9 %psum.23 = f32[64,64]{0,1:T(8,128)S(1)} all-reduce(f32[64,64]{0,1:T(8,128)S(1)} %fusion.73), channel_id=1, replica_groups=mesh['shift'=4,'space'=128] {'shift','space'}, use_global_device_ids=true, to_apply=%region_4.5 | all-reduce | flops 4096 | bytes 32768 | tf_op jit(solution)/shard_map/psum | solution.py:135
  779.5 0.1 copy.40
  779.6 5.8 cholesky.16
  785.5 0.6 compare_reduce_fusion
  786.1 1.3 select_bitcast_fusion
  787.4 4.9 custom-call.6
  792.3 0.1 copy.41
  792.4 0.3 copy.47
  792.7 1.6 fusion.34
  794.3 1.3 copy.43
  795.6 0.6 multiply_add_fusion.3
  (18 shorter events, 0.1 us)
Async XLA Ops:
  7.2 12.7 %copy-start.5 = (f32[8]{0:T(128)S(1)}, f32[8]{0:T(128)}, u32[]{:S(2)}) copy-start(f32[8]{0:T(128)} %param.7) | copy-start | bytes 100
  7.2 12.7 %copy-start.4 = (f32[8]{0:T(128)S(1)}, f32[8]{0:T(128)}, u32[]{:S(2)}) copy-start(f32[8]{0:T(128)} %param.6) | copy-start | bytes 100
  7.2 12.7 %copy-start.3 = (s32[2,32,256]{2,1,0:T(8,128)S(1)}, s32[2,32,256]{2,1,0:T(8,128)}, u32[]{:S(2)}) copy-start(s32[2,32,256]{2,1,0:T(8,128)} %param.5) | copy-start | bytes 196612
  7.2 15.5 %copy-start.6 = (f32[8]{0:T(128)S(1)}, f32[8]{0:T(128)}, u32[]{:S(2)}) copy-start(f32[8]{0:T(128)} %param.8) | copy-start | bytes 100
  9.5 26.2 %all-to-all-start = ((f32[64,2,8,256]{3,2,1,0:T(8,128)}), f32[64,2,8,256]{3,2,1,0:T(8,128)S(1)}, u32[]{:S(2)}, u32[]{:S(2)}) async-start(f32[64,2,8,256]{3,2,1,0:T(8,128)} %slice.133), calls=%async_computation | async-start | bytes 2097152 | tf_op jit(solution)/shard_map/all_to_all | solution.py:119
  20.1 13.0 %collective-permute-start = (f32[1,32,256]{2,1,0:T(8,128)S(1)}, f32[1,32,256]{2,1,0:T(8,128)S(1)}, u32[]{:S(2)}, u32[]{:S(2)}) collective-permute-start(f32[1,32,256]{2,1,0:T(8,128)S(1)} %get-tuple-element.42), channel_id=1, source_target_pairs={{0,1},{1,2},{2,3},{3,4},{4,5},{5,6},{6,7},{7,8},{8,9},{9,10},{10,1... | collective-permute-start | bytes 98312 | tf_op jit(solution)/shard_map/ppermute | solution.py:20
  21.4 11.7 %collective-permute-start.1 = (f32[1,32,256]{2,1,0:T(8,128)S(1)}, f32[1,32,256]{2,1,0:T(8,128)S(1)}, u32[]{:S(2)}, u32[]{:S(2)}) collective-permute-start(f32[1,32,256]{2,1,0:T(8,128)S(1)} %get-tuple-element.43), channel_id=1, source_target_pairs={{1,0},{2,1},{3,2},{4,3},{5,4},{6,5},{7,6},{8,7},{9,8},{10,9},{11,1... | collective-permute-start | bytes 98312 | tf_op jit(solution)/shard_map/ppermute | solution.py:22
  36.1 23.7 %collective-permute-start.2 = (f32[2,8,1,32,256]{4,3,2,1,0:T(8,128)S(1)}, f32[2,8,1,32,256]{4,3,2,1,0:T(8,128)S(1)}, u32[]{:S(2)}, u32[]{:S(2)}) collective-permute-start(f32[2,8,1,32,256]{4,3,2,1,0:T(8,128)S(1)} %get-tuple-element.37), channel_id=1, source_target_pairs={{0,1},{1,2},{2,3},{3,4},{4,5},{5,6},{6,7},{7,8},{8,9},{9,10},{10,1... | collective-permute-start | bytes 1572872 | tf_op jit(solution)/shard_map/ppermute | solution.py:20
  37.9 21.9 %collective-permute-start.3 = (f32[2,8,1,32,256]{4,3,2,1,0:T(8,128)S(1)}, f32[2,8,1,32,256]{4,3,2,1,0:T(8,128)S(1)}, u32[]{:S(2)}, u32[]{:S(2)}) collective-permute-start(f32[2,8,1,32,256]{4,3,2,1,0:T(8,128)S(1)} %get-tuple-element.38), channel_id=1, source_target_pairs={{1,0},{2,1},{3,2},{4,3},{5,4},{6,5},{7,6},{8,7},{9,8},{10,9},{11,1... | collective-permute-start | bytes 1572872 | tf_op jit(solution)/shard_map/ppermute | solution.py:22
  62.9 25.1 %collective-permute-start.4 = (f32[2,8,1,32,256]{4,3,2,1,0:T(8,128)S(1)}, f32[2,8,1,32,256]{4,3,2,1,0:T(8,128)S(1)}, u32[]{:S(2)}, u32[]{:S(2)}) collective-permute-start(f32[2,8,1,32,256]{4,3,2,1,0:T(8,128)S(1)} %get-tuple-element.35), channel_id=1, source_target_pairs={{0,1},{1,2},{2,3},{3,4},{4,5},{5,6},{6,7},{7,8},{8,9},{9,10},{10,1... | collective-permute-start | bytes 1572872 | tf_op jit(solution)/shard_map/ppermute | solution.py:20
  67.1 20.9 %collective-permute-start.5 = (f32[2,8,1,32,256]{4,3,2,1,0:T(8,128)S(1)}, f32[2,8,1,32,256]{4,3,2,1,0:T(8,128)S(1)}, u32[]{:S(2)}, u32[]{:S(2)}) collective-permute-start(f32[2,8,1,32,256]{4,3,2,1,0:T(8,128)S(1)} %get-tuple-element.36), channel_id=1, source_target_pairs={{1,0},{2,1},{3,2},{4,3},{5,4},{6,5},{7,6},{8,7},{9,8},{10,9},{11,1... | collective-permute-start | bytes 1572872 | tf_op jit(solution)/shard_map/ppermute | solution.py:22
  91.1 24.0 %collective-permute-start.6 = (f32[2,8,1,32,256]{4,3,2,1,0:T(8,128)S(1)}, f32[2,8,1,32,256]{4,3,2,1,0:T(8,128)S(1)}, u32[]{:S(2)}, u32[]{:S(2)}) collective-permute-start(f32[2,8,1,32,256]{4,3,2,1,0:T(8,128)S(1)} %get-tuple-element.33), channel_id=1, source_target_pairs={{0,1},{1,2},{2,3},{3,4},{4,5},{5,6},{6,7},{7,8},{8,9},{9,10},{10,1... | collective-permute-start | bytes 1572872 | tf_op jit(solution)/shard_map/ppermute | solution.py:20
  95.3 19.9 %collective-permute-start.7 = (f32[2,8,1,32,256]{4,3,2,1,0:T(8,128)S(1)}, f32[2,8,1,32,256]{4,3,2,1,0:T(8,128)S(1)}, u32[]{:S(2)}, u32[]{:S(2)}) collective-permute-start(f32[2,8,1,32,256]{4,3,2,1,0:T(8,128)S(1)} %get-tuple-element.34), channel_id=1, source_target_pairs={{1,0},{2,1},{3,2},{4,3},{5,4},{6,5},{7,6},{8,7},{9,8},{10,9},{11,1... | collective-permute-start | bytes 1572872 | tf_op jit(solution)/shard_map/ppermute | solution.py:22
  120.1 22.0 %all-to-all-start.1 = ((f32[16,2,32,256]{3,1,0,2:T(2,128)}), f32[16,2,32,256]{3,1,0,2:T(2,128)S(1)}, u32[]{:S(2)}, u32[]{:S(2)}) async-start(f32[16,2,32,256]{3,1,0,2:T(2,128)} %copy.36), calls=%async_computation.1 | async-start | bytes 2097152 | tf_op jit(solution)/shard_map/all_to_all | solution.py:129
  127.0 290.7 %all-reduce.7.cloned.1.call-start = ((), (), s32[]{:S(2)}) async-start(), calls=%async_computation.2 | async-start | bytes 131072 | tf_op jit(solution)/shard_map/psum | solution.py:131
  149.9 528.9 %all-reduce.9.cloned.1.call-start = ((), (), s32[]{:S(2)}) async-start(), calls=%async_computation.3 | async-start | bytes 131072 | tf_op jit(solution)/shard_map/psum | solution.py:133
  417.8 5.0 copy-start
  684.6 111.0 %copy-start.1 = (f32[64,256]{1,0:T(8,128)S(1)}, f32[64,256]{1,0:T(8,128)}, u32[]{:S(2)}) copy-start(f32[64,256]{1,0:T(8,128)} %all-reduce.7.cloned.1.call-done) | copy-start | bytes 196612
  684.6 111.0 %copy-start.2 = (f32[64,256]{1,0:T(8,128)S(1)}, f32[64,256]{1,0:T(8,128)}, u32[]{:S(2)}) copy-start(f32[64,256]{1,0:T(8,128)} %all-reduce.9.cloned.1.call-done) | copy-start | bytes 196612
Sparse Core Ops, SparseCore 0:
  150.0 267.6 all-reduce.6
  427.5 251.2 all-reduce.8
where the time goes:
time: 804 us; the launch traced here: 803 us
  waiting for transfers between devices  598 us (74%)
  blocking collectives  94.9 us (12%)
  starting transfers between devices  34.2 us (4%)
  matrix products  23.7 us (3%)
  other arithmetic  23.2 us (3%)
  local copies, waits for them, and re-layouts  15.2 us (2%)
  between operations  14.3 us (2%)
    psum x2, waiting for transfers between devices, local(): lax.psum(products(columns, flat_basis), ('shift', 'space')) * cell_weight  519 us
    psum x1, blocking collectives, local(): lax.psum(products(columns, columns), ('shift', 'space')) * cell_weight  94.9 us
    ppermute x4, waiting for transfers between devices, padded_2(): lax.ppermute(tail, axis, [(i, (i + 1) % count) for i in range(ends)])  69 us
  transfers between devices with their start and end apart: 12, of which 8 were waited for; matrix products, arithmetic and copies ran while one was open for 1% of the time, Pallas kernels for 0%

commit v1 on v0

--- a/solution.py
+++ b/solution.py
@@ -128,7 +128,10 @@
     merged = fields.reshape(per_device * COLS, slab_x, full_y, depth)
     regrouped = lax.all_to_all(merged, "shift", split_axis=2, concat_axis=0, tiled=True)
     columns = regrouped.reshape(new_count, slab_x * quarter * depth)
-    first_proj = lax.psum(products(columns, flat_basis), ("shift", "space")) * cell_weight
+    first_proj = (
+        jnp.sum(lax.all_gather(products(columns, flat_basis), ("shift", "space")), axis=0)
+        * cell_weight
+    )
     columns = columns - matmul(first_proj, flat_basis)
     second_proj = lax.psum(products(columns, flat_basis), ("shift", "space")) * cell_weight
     columns = columns - matmul(second_proj, flat_basis)

time: 804 us -> 2030 us (2.52)
  waiting for transfers between devices: 598 us -> 1810 us
    all_gather x0 -> x1, waiting for transfers between devices: none -> 1470 us  [local(): lax.all_gather(products(columns, flat_basis), ('shift', 'space'))]
    psum x2 -> x1, waiting for transfers between devices: 519 us -> 262 us  [local(): lax.psum(products(columns, flat_basis), ('shift', 'space')) * cell_weight]
  transfers between devices with their start and end apart: 12 -> 12, of which waited for: 8 -> 8; matrix products, arithmetic and copies ran while one was open for 1% -> 0% of each run, Pallas kernels for 0% -> 0%
where the time goes in v1:
time: 2030 us
  waiting for transfers between devices  1810 us (89%)
  blocking collectives  94.9 us (5%)
  other arithmetic  36.1 us (2%)
  starting transfers between devices  34.2 us (2%)
  matrix products  23.7 us (1%)
    all_gather x1, waiting for transfers between devices, local(): lax.all_gather(products(columns, flat_basis), ('shift', 'space'))  1470 us
    psum x1, waiting for transfers between devices, local(): lax.psum(products(columns, flat_basis), ('shift', 'space')) * cell_weight  262 us
    psum x1, blocking collectives, local(): lax.psum(products(columns, columns), ('shift', 'space')) * cell_weight  94.9 us
    ppermute x4, waiting for transfers between devices, padded_2(): lax.ppermute(tail, axis, [(i, (i + 1) % count) for i in range(ends)])  69 us
  transfers between devices with their start and end apart: 12, of which 8 were waited for; matrix products, arithmetic and copies ran while one was open for 0% of the time, Pallas kernels for 0%

profile of v1, /device:TPU:1, one launch (start us, length us, event | category | flops | bytes accessed | tf_op | source)
XLA Modules:
  0.0 2027.0 jit_solution(7498677983524243202)
XLA Ops:
  7.2 2.3 slice.133
  9.5 10.4 all-to-all-start
  19.9 0.2 select_reduce_fusion.1
  20.1 1.3 collective-permute-start
  21.4 1.3 collective-permute-start.1
  22.7 0.1 dynamic_slice.3
  22.8 10.3 collective-permute-done
  33.0 0.0 collective-permute-done.1
  33.0 0.1 select_maximum_fusion.6
  33.2 0.1 add_add_fusion
  33.3 0.1 multiply_add_fusion.2
  33.4 2.3 all-to-all-done
  35.7 0.1 copy.35
  35.8 0.1 fusion.37
  36.0 0.1 fusion.69
  36.1 1.9 collective-permute-start.2
  37.9 1.3 collective-permute-start.3
  39.2 20.6 %collective-permute-done.2 = f32[2,8,1,32,256]{4,3,2,1,0:T(8,128)S(1)} collective-permute-done((f32[2,8,1,32,256]{4,3,2,1,0:T(8,128)S(1)}, f32[2,8,1,32,256]{4,3,2,1,0:T(8,128)S(1)}, u32[]{:S(2)}, u32[]{:S(2)}) %collective-permute-start.2) | collective-permute-done | bytes 524320 | tf_op jit(solution)/shard_map/ppermute | solution.py:20
  59.8 0.0 collective-permute-done.3
  59.8 1.8 select_maximum_fusion.4
  61.6 1.2 multiply_add_fusion.1
  62.8 0.1 fusion.68
  62.9 4.1 collective-permute-start.4
  67.1 1.3 collective-permute-start.5
  68.4 19.6 collective-permute-done.4
  88.0 0.0 collective-permute-done.5
  88.0 1.8 select_maximum_fusion.2
  89.9 1.2 multiply_add_fusion
  91.0 0.1 fusion.67
  91.1 4.1 collective-permute-start.6
  95.2 1.3 collective-permute-start.7
  96.5 18.6 collective-permute-done.6
  115.1 0.0 collective-permute-done.7
  115.1 1.8 select_maximum_fusion
  116.9 1.4 fusion.9
  118.3 1.8 copy.36
  120.1 6.9 all-to-all-start.1
  127.0 8.0 copy.46
  135.1 7.1 all-to-all-done.1
  142.1 0.6 copy.53
  142.7 0.1 copy.38
  142.9 0.2 reshape.60
  143.1 6.8 fusion.71
  149.9 0.0 all-gather.3.cloned.1.call-update
  149.9 0.3 all-reduce.6.cloned.1.call-start
  150.2 1468.3 %all-gather.3.cloned.1.call-done = f32[32768,256]{1,0:T(8,128)} async-done(((f32[64,256]{1,0:T(8,128)}), f32[32768,256]{1,0:T(8,128)}) %all-gather.3.cloned.1.call-update) | async-done | bytes 33554448 | tf_op jit(solution)/shard_map/all_gather | solution.py:132
  1618.4 12.9 reduce_sum.29
  1631.4 5.0 convolution_subtract_fusion.1
  1636.3 4.6 fusion.72
  1640.9 0.0 all-reduce.6.cloned.1.call-update
  1641.0 261.8 %all-reduce.6.cloned.1.call-done = f32[64,256]{1,0:T(8,128)} async-done(((f32[64,256]{1,0:T(8,128)}), f32[64,256]{1,0:T(8,128)}) %all-reduce.6.cloned.1.call-update) | async-done | bytes 65552 | tf_op jit(solution)/shard_map/psum | solution.py:136
  1902.7 4.8 convolution_subtract_fusion
  1907.6 1.0 fusion.73
  1908.6 94.9 %psum.15 = f32[64,64]{0,1:T(8,128)S(1)} all-reduce(f32[64,64]{0,1:T(8,128)S(1)} %fusion.73), channel_id=1, replica_groups=mesh['shift'=4,'space'=128] {'shift','space'}, use_global_device_ids=true, to_apply=%region_4.5 | all-reduce | flops 4096 | bytes 32768 | tf_op jit(solution)/shard_map/psum | solution.py:138
  2003.5 0.1 copy.40
  2003.6 5.8 cholesky.16
  2009.4 0.6 compare_reduce_fusion
  2010.1 1.3 select_bitcast_fusion
  2011.3 4.9 custom-call.6
  2016.2 0.1 copy.41
  2016.3 0.3 copy.47
  2016.7 1.6 fusion.34
  2018.3 1.3 copy.43
  2019.6 0.6 multiply_add_fusion.3
  (17 shorter events, 0.1 us)
Async XLA Ops:
  7.2 12.7 copy-start.4
  7.2 12.7 copy-start.3
  7.2 12.7 copy-start.2
  7.2 15.5 copy-start.5
  9.5 26.2 %all-to-all-start = ((f32[64,2,8,256]{3,2,1,0:T(8,128)}), f32[64,2,8,256]{3,2,1,0:T(8,128)S(1)}, u32[]{:S(2)}, u32[]{:S(2)}) async-start(f32[64,2,8,256]{3,2,1,0:T(8,128)} %slice.133), calls=%async_computation | async-start | bytes 2097152 | tf_op jit(solution)/shard_map/all_to_all | solution.py:119
  20.1 13.0 collective-permute-start
  21.4 11.7 collective-permute-start.1
  36.1 23.7 %collective-permute-start.2 = (f32[2,8,1,32,256]{4,3,2,1,0:T(8,128)S(1)}, f32[2,8,1,32,256]{4,3,2,1,0:T(8,128)S(1)}, u32[]{:S(2)}, u32[]{:S(2)}) collective-permute-start(f32[2,8,1,32,256]{4,3,2,1,0:T(8,128)S(1)} %get-tuple-element.37), channel_id=1, source_target_pairs={{0,1},{1,2},{2,3},{3,4},{4,5},{5,6},{6,7},{7,8},{8,9},{9,10},{10,1... | collective-permute-start | bytes 1572872 | tf_op jit(solution)/shard_map/ppermute | solution.py:20
  37.9 21.9 %collective-permute-start.3 = (f32[2,8,1,32,256]{4,3,2,1,0:T(8,128)S(1)}, f32[2,8,1,32,256]{4,3,2,1,0:T(8,128)S(1)}, u32[]{:S(2)}, u32[]{:S(2)}) collective-permute-start(f32[2,8,1,32,256]{4,3,2,1,0:T(8,128)S(1)} %get-tuple-element.38), channel_id=1, source_target_pairs={{1,0},{2,1},{3,2},{4,3},{5,4},{6,5},{7,6},{8,7},{9,8},{10,9},{11,1... | collective-permute-start | bytes 1572872 | tf_op jit(solution)/shard_map/ppermute | solution.py:22
  62.9 25.1 %collective-permute-start.4 = (f32[2,8,1,32,256]{4,3,2,1,0:T(8,128)S(1)}, f32[2,8,1,32,256]{4,3,2,1,0:T(8,128)S(1)}, u32[]{:S(2)}, u32[]{:S(2)}) collective-permute-start(f32[2,8,1,32,256]{4,3,2,1,0:T(8,128)S(1)} %get-tuple-element.35), channel_id=1, source_target_pairs={{0,1},{1,2},{2,3},{3,4},{4,5},{5,6},{6,7},{7,8},{8,9},{9,10},{10,1... | collective-permute-start | bytes 1572872 | tf_op jit(solution)/shard_map/ppermute | solution.py:20
  67.1 20.9 %collective-permute-start.5 = (f32[2,8,1,32,256]{4,3,2,1,0:T(8,128)S(1)}, f32[2,8,1,32,256]{4,3,2,1,0:T(8,128)S(1)}, u32[]{:S(2)}, u32[]{:S(2)}) collective-permute-start(f32[2,8,1,32,256]{4,3,2,1,0:T(8,128)S(1)} %get-tuple-element.36), channel_id=1, source_target_pairs={{1,0},{2,1},{3,2},{4,3},{5,4},{6,5},{7,6},{8,7},{9,8},{10,9},{11,1... | collective-permute-start | bytes 1572872 | tf_op jit(solution)/shard_map/ppermute | solution.py:22
  91.1 24.0 %collective-permute-start.6 = (f32[2,8,1,32,256]{4,3,2,1,0:T(8,128)S(1)}, f32[2,8,1,32,256]{4,3,2,1,0:T(8,128)S(1)}, u32[]{:S(2)}, u32[]{:S(2)}) collective-permute-start(f32[2,8,1,32,256]{4,3,2,1,0:T(8,128)S(1)} %get-tuple-element.33), channel_id=1, source_target_pairs={{0,1},{1,2},{2,3},{3,4},{4,5},{5,6},{6,7},{7,8},{8,9},{9,10},{10,1... | collective-permute-start | bytes 1572872 | tf_op jit(solution)/shard_map/ppermute | solution.py:20
  95.2 19.9 collective-permute-start.7
  120.1 22.0 %all-to-all-start.1 = ((f32[16,2,32,256]{3,1,0,2:T(2,128)}), f32[16,2,32,256]{3,1,0,2:T(2,128)S(1)}, u32[]{:S(2)}, u32[]{:S(2)}) async-start(f32[16,2,32,256]{3,1,0,2:T(2,128)} %copy.36), calls=%async_computation.1 | async-start | bytes 2097152 | tf_op jit(solution)/shard_map/all_to_all | solution.py:129
  127.0 1491.4 %all-gather.3.cloned.1.call-start = ((), (), s32[]{:S(2)}) async-start(), calls=%async_computation.3 | async-start | bytes 33619968 | tf_op jit(solution)/shard_map/all_gather | solution.py:132
  149.9 1752.9 %all-reduce.6.cloned.1.call-start = ((), (), s32[]{:S(2)}) async-start(), calls=%async_computation.2 | async-start | bytes 131072 | tf_op jit(solution)/shard_map/psum | solution.py:136
  1631.4 5.0 copy-start
  1908.6 111.0 %copy-start.1 = (f32[64,256]{1,0:T(8,128)S(1)}, f32[64,256]{1,0:T(8,128)}, u32[]{:S(2)}) copy-start(f32[64,256]{1,0:T(8,128)} %all-reduce.6.cloned.1.call-done) | copy-start | bytes 196612
Sparse Core Ops, SparseCore 0:
  150.0 1468.3 all-gather.2
  1641.1 261.6 all-reduce.5
